TPU v7x, 32 devices: a whole 2x2x4 slice. The times are simulated.
32 devices in a mesh: freq: 2 (over y), clus: 4 (over z), src: 2 (over x), sub: 2 (over core).
Axes of the slice: x: 2, y: 2, z: 4, core: 2. Of those that a mesh axis runs over, the one named last changes fastest.
Arguments:
- charges: bfloat16 [512, 48, 128], P(('freq', 'src'), 'clus'), parts along dimension 0, may hold values from -6 to 6
- geometry: float32 [4, 48, 256], replicated, may hold values from -4 to 4, as said below
- wavenumber: float32 [2], P('freq'), parts along dimension 0, may hold values from 0.3 to 2
- requests: int32 [8, 4, 4], P(('clus', 'sub')), may hold values from -1 to 11, as said below
- pairs: int32 [48, 2, 32], P('clus', 'sub'), may hold values from 0 to 15, as said below
- counts: int32 [48, 2], P('clus', 'sub'), may hold values from 1 to 32, as said below
Outputs:
- iterate: bfloat16 [512, 48, 128], P(('freq', 'src'), 'clus'), parts along dimension 0
- image: float32 [512, 48, 128], P(('freq', 'src', 'sub'), 'clus'), parts along dimension 0
There are 2 independent parts, one for each index of `freq`. A program takes and returns all parts, laid end to end along the dimension named above; an argument that names none is the same for every part. Nothing has to cross between parts.
Inputs may be any that keep to these rules, and one draw needn't show every extreme that they name: `geometry`: rows: x and y, depth z from -1 to -0.05, panel area from 0.05 to 0.5. `requests`: each row's live entries are distinct cluster numbers and come first, -1 marks an empty slot; in every block the row of the block's own clus index holds 4 live entries. `pairs`: every entry d * 4 + k names a live entry requests[b, d, k] of the block b of the target cluster's owner and half. `counts`: 32 is reached in every draw.
All inputs are finite; a program needn't handle non-finite values.
Results may differ from a plain program's by a relative error of at most 0.0049.
Values may be sent and summed in bfloat16 or wider, within the bound.
No kernel may reach another device: no remote copies, remote signals or barrier semaphores. Data moves between devices by JAX's collectives and lax.ppermute only.
A program may use at most 64 MiB of HBM per device.

v0:
```python
import jax
import jax.numpy as jnp
from jax import lax
from jax.experimental import pallas as pl
from jax.experimental.pallas import tpu as pltpu
from jax.sharding import PartitionSpec as P

CPD = 12
CAP = 4
PPT = 32

quarter_turn = 0.7853981633974483
two_pi = 6.283185307179586
inverse_four_pi = 0.07957747154594767
inverse_pi = 0.3183098861837907
SIN_A = (-0.16666661577130884, 0.008333118573140752, -0.00019813475437141734, 2.6144256303410747e-06)
COS_B = (
    -0.4999999981796688,
    0.041666651863571776,
    -0.0013888547499597086,
    2.4769209821955003e-05,
    -2.620509973872218e-07,
)

STRIP = 16
LANES = 128
UNROLL = 4


def green(k, xt, yt, zt, zt4, et, xs, ys, zs, area, sj, cj):
    dx = xt - xs
    dy = yt - ys
    planar = dx * dx + dy * dy
    dz = zt - zs
    near = planar + dz * dz + area
    direct = lax.rsqrt(near)
    mirror = lax.rsqrt(near + zt4 * zs)
    kr = k * (planar * lax.rsqrt(jnp.maximum(planar, 1e-30)))
    amp = (et * cj) * lax.rsqrt(1.0 + kr)
    phase = kr + quarter_turn
    n = jnp.floor(phase * inverse_pi + 0.5)
    r = (phase - n * 3.140625) - n * 0.0009676535846665502
    z = r * r
    sin = r + r * (z * (SIN_A[0] + z * (SIN_A[1] + z * (SIN_A[2] + z * SIN_A[3]))))
    cos = 1.0 + z * (COS_B[0] + z * (COS_B[1] + z * (COS_B[2] + z * (COS_B[3] + z * COS_B[4]))))
    amp = jnp.where((n.astype(jnp.int32) & 1) == 1, -amp, amp)
    return sj * (direct + mirror) - amp * sin, amp * cos


def tile_into(k, tb_ref, sb_ref, g, p, tr_ref, ti_ref):
    width = tr_ref.shape[0]
    halves = tr_ref.shape[1] // LANES

    def strip(r, carry):
        rows = pl.ds(pl.multiple_of(r * STRIP, STRIP), STRIP)
        xs = sb_ref[p, 0, rows, :]
        ys = sb_ref[p, 1, rows, :]
        zs = sb_ref[p, 2, rows, :]
        area = sb_ref[p, 3, rows, :]
        sj = sb_ref[p, 4, rows, :]
        cj = sb_ref[p, 5, rows, :]
        for h in range(halves):
            lanes = pl.ds(h * LANES, LANES)
            xt = tb_ref[g, 0, :, lanes]
            yt = tb_ref[g, 1, :, lanes]
            zt = tb_ref[g, 2, :, lanes]
            et = tb_ref[g, 3, :, lanes]
            zt4 = tb_ref[g, 4, :, lanes]
            re, im = green(k, xt, yt, zt, zt4, et, xs, ys, zs, area, sj, cj)
            tr_ref[rows, lanes] = re.astype(jnp.bfloat16)
            ti_ref[rows, lanes] = im.astype(jnp.bfloat16)
        return carry

    lax.fori_loop(0, width // STRIP, strip, 0, unroll=UNROLL)


def entry_product(l_ref, p, tile):
    return jnp.dot(l_ref[p], tile, preferred_element_type=jnp.float32)


def product_kernel(w_ref, k_ref, tb_ref, sb_ref, l_ref, acc_ref, tbuf):
    k = k_ref[0]
    slots = sb_ref.shape[0]
    width = tbuf.shape[0] // 2
    acc_ref[...] = jnp.zeros_like(acc_ref)

    def body(e, carry):
        w = w_ref[e]

        @pl.when(w > 0.0)
        def _():
            g = e // slots
            p = e % slots
            tile_into(k, tb_ref, sb_ref, g, p, tbuf.at[pl.ds(0, width)], tbuf.at[pl.ds(width, width)])
            part = entry_product(l_ref, p, tbuf[...])
            acc_ref[g] = acc_ref[g] + w * part

        return carry

    lax.fori_loop(0, w_ref.shape[0], body, 0)


SMEM_SPEC = pl.BlockSpec(memory_space=pltpu.SMEM)
VMEM_SPEC = pl.BlockSpec(memory_space=pltpu.VMEM)


def product(w_list, k, tb, sb, lhs):
    clusters = tb.shape[0]
    targets = tb.shape[3]
    width = sb.shape[2]
    cols = lhs.shape[1]
    elems = clusters * width * targets * PPT
    return pl.pallas_call(
        product_kernel,
        out_shape=jax.ShapeDtypeStruct((clusters, cols, targets), jnp.float32),
        in_specs=[SMEM_SPEC] * 2 + [VMEM_SPEC] * 3,
        out_specs=VMEM_SPEC,
        scratch_shapes=[pltpu.VMEM((2 * width, targets), jnp.bfloat16)],
        cost_estimate=pl.CostEstimate(
            flops=elems * 60 + 4 * elems * cols,
            transcendentals=elems * 4,
            bytes_accessed=elems * 2,
        ),
    )(w_list, k, tb, sb, lhs)


def scatter_sum(x, axis):
    count = lax.axis_size(axis)
    if count == 1:
        return x
    me = lax.axis_index(axis)
    blocks = x.reshape((count, x.shape[0] // count) + x.shape[1:])
    total = lax.dynamic_index_in_dim(blocks, me, 0, keepdims=False)
    for shift in range(1, count):
        send = lax.dynamic_index_in_dim(blocks, (me + shift) % count, 0, keepdims=False)
        perm = [(i, (i + shift) % count) for i in range(count)]
        total = total + lax.ppermute(send, axis, perm=perm)
    return total


def local(charges, geometry, wavenumber, requests, pairs, counts):
    clus_index = lax.axis_index("clus")
    src_index = lax.axis_index("src")
    sub_index = lax.axis_index("sub")
    clus_count = lax.axis_size("clus")
    sub_count = lax.axis_size("sub")
    source_rows = charges.shape[0]
    share_rows = source_rows // sub_count
    targets = geometry.shape[2]
    cpd = charges.shape[1]
    wavenum = wavenumber[0]
    slot_total = clus_count * requests.shape[2]

    def swap_chunks(x, axis):
        by_shift = [lax.dynamic_index_in_dim(x, clus_index, axis, keepdims=False)]
        for shift in range(1, clus_count):
            send = lax.dynamic_index_in_dim(x, (clus_index + shift) % clus_count, axis, False)
            perm = [(i, (i + shift) % clus_count) for i in range(clus_count)]
            by_shift.append(lax.ppermute(send, "clus", perm=perm))
        stacked = jnp.stack(by_shift, axis=axis)
        return jnp.take(stacked, (clus_index - jnp.arange(clus_count)) % clus_count, axis=axis)

    served = swap_chunks(requests[0], 0).reshape(-1)
    served_index = jnp.maximum(served, 0)
    served_mask = (served >= 0).astype(jnp.bfloat16)[None, :, None]

    def fetch(values):
        picked = jnp.take(values, served_index, axis=1) * served_mask
        chunks = picked.reshape(
            (picked.shape[0], clus_count, picked.shape[1] // clus_count) + picked.shape[2:]
        )
        return swap_chunks(chunks, 1).reshape(picked.shape)

    def lhs_of(values):
        blocks = fetch(values)
        half_width = blocks.shape[2] // 2
        swapped = jnp.concatenate([-blocks[..., half_width:], blocks[..., :half_width]], axis=-1)
        return jnp.concatenate(
            [jnp.transpose(blocks, (1, 2, 0)), jnp.transpose(swapped, (1, 2, 0))], axis=2
        )

    target_geo = lax.dynamic_slice_in_dim(geometry, clus_index * cpd, cpd, axis=1)
    base = jnp.concatenate([target_geo[:3], target_geo[2:3], target_geo[2:3]], axis=0)
    row = jnp.arange(5, dtype=jnp.int32)[:, None, None]
    tq = jnp.where(row == 3, jnp.exp(wavenum * base), jnp.where(row == 4, 4.0 * base, base))
    tb = jnp.broadcast_to(
        jnp.transpose(tq, (1, 0, 2))[:, :, None, :], (cpd, tq.shape[0], STRIP, targets)
    )

    base_ids = jnp.arange(clus_count, dtype=jnp.int32)[:, None] * cpd
    source_ids = (base_ids + jnp.maximum(requests[0], 0)).reshape(-1)
    source_full = jnp.take(geometry, source_ids, axis=1)
    source_geo = lax.dynamic_slice_in_dim(source_full, src_index * source_rows, source_rows, axis=2)
    sj = source_geo[3] * inverse_four_pi
    cj = (two_pi * wavenum) * jnp.exp(wavenum * source_geo[2]) * sj
    sq = jnp.stack([source_geo[0], source_geo[1], source_geo[2], source_geo[3], sj, cj], axis=1)
    sb = jnp.broadcast_to(sq[..., None], sq.shape + (LANES,))

    slot_ids = pairs[:, 0, :]
    live = jnp.arange(pairs.shape[2], dtype=jnp.int32)[None, :] < counts[:, 0:1]
    hits = (slot_ids[:, :, None] == jnp.arange(slot_total, dtype=jnp.int32)[None, None, :]) & live[
        :, :, None
    ]
    w_list = jnp.sum(hits.astype(jnp.float32), axis=1).reshape(-1)
    k_arr = wavenumber.astype(jnp.float32).reshape(1)

    src_count = lax.axis_size("src")

    def finish(acc):
        clusters, cols, _ = acc.shape
        rows = targets // (src_count * sub_count)
        split = acc.reshape(clusters, cols, src_count, sub_count, rows)
        ordered = jnp.transpose(split, (3, 2, 4, 0, 1)).reshape(targets, clusters, cols)
        return scatter_sum(scatter_sum(ordered, "sub"), "src")

    first = finish(product(w_list, k_arr, tb, sb, lhs_of(charges)))
    own_rows = lax.dynamic_slice_in_dim(charges, sub_index * share_rows, share_rows, axis=0)
    iterate_share = (own_rows.astype(jnp.float32) - first).astype(jnp.bfloat16)
    iterate = lax.all_gather(iterate_share, "sub", axis=0, tiled=True)
    image = finish(product(w_list, k_arr, tb, sb, lhs_of(iterate)))
    return (iterate, image)


def solution(mesh):
    in_specs = (
        P(("freq", "src"), "clus", None),
        P(),
        P("freq"),
        P(("clus", "sub"), None, None),
        P("clus", "sub", None),
        P("clus", "sub"),
    )
    out_specs = (P(("freq", "src"), "clus", None), P(("freq", "src", "sub"), "clus", None))
    return jax.shard_map(local, mesh=mesh, in_specs=in_specs, out_specs=out_specs, check_vma=False)
```

profile of v0, /device:TPU:8, one launch (start us, length us, event | category | flops | bytes accessed | tf_op | source)
XLA Modules:
  0.0 184.9 jit_solution(2301581830333134511)
XLA Ops:
  0.7 0.8 fusion.11
  1.5 1.6 collective-permute-start
  3.1 1.1 collective-permute-start.1
  4.2 2.0 %collective-permute-start.2 = (s32[4]{0:T(128)S(1)}, s32[4]{0:T(128)S(1)}, u32[]{:S(2)}, u32[]{:S(2)}) collective-permute-start(s32[4]{0:T(128)S(1)} %get-tuple-element.18), channel_id=1, source_target_pairs={{0,12},{4,0},{8,4},{12,8},{1,13},{5,1},{9,5},{13,9},{2,14},{6,2},{... | collective-permute-start | bytes 56 | tf_op jit(solution)/shard_map/ppermute | solution.py:159
  6.2 0.7 broadcast_maximum_fusion
  8.2 0.7 copy.28
  8.9 0.7 iota_compare_fusion.1
  9.7 0.6 reshape.241.w_ref
  10.4 0.6 gather_fusion.1
  11.3 1.6 gather_fusion.2
  13.0 0.1 bitcast_multiply_fusion.1
  13.3 3.6 %collective-permute-start.4 = (bf16[128,4,128]{2,0,1:T(8,128)(2,1)S(1)}, bf16[128,4,128]{2,0,1:T(8,128)(2,1)S(1)}, u32[]{:S(2)}, u32[]{:S(2)}) collective-permute-start(bf16[128,4,128]{2,0,1:T(8,128)(2,1)S(1)} %get-tuple-element.14), channel_id=1, source_target_pairs={{0,8},{4,12},{8,0},{12,4},{1,9},{5,13},{9,1},{13,5},{2,10},{6,14},... | collective-permute-start | bytes 393224 | tf_op jit(solution)/shard_map/ppermute | solution.py:159
  16.9 0.6 gather_fusion
  17.8 1.9 %collective-permute-done.3 = bf16[128,4,128]{2,0,1:T(8,128)(2,1)S(1)} collective-permute-done((bf16[128,4,128]{2,0,1:T(8,128)(2,1)S(1)}, bf16[128,4,128]{2,0,1:T(8,128)(2,1)S(1)}, u32[]{:S(2)}, u32[]{:S(2)}) %collective-permute-start.3) | collective-permute-done | bytes 131104 | tf_op jit(solution)/shard_map/ppermute | solution.py:159
  19.7 4.5 %collective-permute-done.4 = bf16[128,4,128]{2,0,1:T(8,128)(2,1)S(1)} collective-permute-done((bf16[128,4,128]{2,0,1:T(8,128)(2,1)S(1)}, bf16[128,4,128]{2,0,1:T(8,128)(2,1)S(1)}, u32[]{:S(2)}, u32[]{:S(2)}) %collective-permute-start.4) | collective-permute-done | bytes 131104 | tf_op jit(solution)/shard_map/ppermute | solution.py:159
  24.2 3.1 %collective-permute-done.5 = bf16[128,4,128]{2,0,1:T(8,128)(2,1)S(1)} collective-permute-done((bf16[128,4,128]{2,0,1:T(8,128)(2,1)S(1)}, bf16[128,4,128]{2,0,1:T(8,128)(2,1)S(1)}, u32[]{:S(2)}, u32[]{:S(2)}) %collective-permute-start.5) | collective-permute-done | bytes 131104 | tf_op jit(solution)/shard_map/ppermute | solution.py:159
  27.4 0.6 gather_fusion.3
  28.0 0.1 select_bitcast_fusion.1
  28.1 0.3 copy.20
  28.5 1.2 pad_maximum_fusion.l_ref
  29.7 3.8 %broadcast_in_dim.70.sb_ref = f32[16,6,128,128]{3,2,1,0:T(8,128)} broadcast(f32[16,6,128]{2,1,0:T(8,128)S(1)} %copy.19), dimensions={0,1,2} | broadcast | bytes 6340608 | tf_op jit(solution)/shard_map/broadcast_in_dim | solution.py:197
  33.5 1.0 broadcast_in_dim.67.tb_ref
  34.5 49.1 %shard_map.80 = f32[12,128,256]{2,1,0:T(8,128)} custom-call(f32[192]{0:T(256)} %reshape.241.w_ref, f32[1]{0:T(128)} %copy.35.k_ref, f32[12,5,16,256]{3,2,1,0:T(8,128)} %broadcast_in_dim.67.tb_ref, f32[16,6,128,128]{3,2,1,0:T(8,128)} %broadcast_in_dim.70.sb_ref, bf16[16,128,256]{2,1,0:T(8,128)(2,1)} %pad_maximum_fusion.l_ref), custom_call_target="tpu_custom_call" | custom-call | flops 7197425664 | bytes 25165824 | tf_op jit(solution)/shard_map/pallas_call | solution.py:113
  83.7 1.9 %copy.21 = f32[12,128,256]{1,2,0:T(8,128)S(1)} copy(f32[12,128,256]{2,1,0:T(8,128)} %shard_map.80) | data formatting | bytes 3145728 | tf_op jit(solution)/shard_map/pallas_call | solution.py:113
  85.5 0.2 copy.22
  85.9 2.4 %collective-permute-done.6 = f32[128,12,128]{2,0,1:T(8,128)} collective-permute-done((f32[128,12,128]{2,0,1:T(8,128)S(1)}, f32[128,12,128]{2,0,1:T(8,128)}, u32[]{:S(2)}, u32[]{:S(2)}) %collective-permute-start.6) | collective-permute-done | bytes 786464 | tf_op jit(solution)/shard_map/ppermute | solution.py:137
  88.3 1.2 bitcast_add_fusion.1
  89.5 1.6 collective-permute-start.7
  91.1 9.7 %collective-permute-done.7 = f32[64,12,128]{2,0,1:T(8,128)S(1)} collective-permute-done((f32[64,12,128]{2,0,1:T(8,128)S(1)}, f32[64,12,128]{2,0,1:T(8,128)S(1)}, u32[]{:S(2)}, u32[]{:S(2)}) %collective-permute-start.7) | collective-permute-done | bytes 393248 | tf_op jit(solution)/shard_map/ppermute | solution.py:137
  100.8 2.1 %all_gather.3 = bf16[128,12,128]{2,0,1:T(8,128)(2,1)S(1)} all-gather(bf16[64,12,128]{2,0,1:T(8,128)(2,1)S(1)} %fusion.1), channel_id=1, replica_groups=mesh['freq'=2,'clus'=4,'src'=2,'sub'=2] {'sub'}, dimensions={0}, use_global_device_ids=true | all-gather | bytes 589824 | tf_op jit(solution)/shard_map/all_gather | solution.py:219
  102.9 0.6 gather_fusion.4
  103.6 0.1 bitcast_multiply_fusion
  103.9 1.9 %collective-permute-start.10 = (bf16[128,4,128]{2,0,1:T(8,128)(2,1)S(1)}, bf16[128,4,128]{2,0,1:T(8,128)(2,1)S(1)}, u32[]{:S(2)}, u32[]{:S(2)}) collective-permute-start(bf16[128,4,128]{2,0,1:T(8,128)(2,1)S(1)} %get-tuple-element.7), channel_id=1, source_target_pairs={{0,12},{4,0},{8,4},{12,8},{1,13},{5,1},{9,5},{13,9},{2,14},{6,2},{... | collective-permute-start | bytes 393224 | tf_op jit(solution)/shard_map/ppermute | solution.py:159
  105.9 4.3 %collective-permute-done.8 = bf16[128,4,128]{2,0,1:T(8,128)(2,1)S(1)} collective-permute-done((bf16[128,4,128]{2,0,1:T(8,128)(2,1)S(1)}, bf16[128,4,128]{2,0,1:T(8,128)(2,1)S(1)}, u32[]{:S(2)}, u32[]{:S(2)}) %collective-permute-start.8) | collective-permute-done | bytes 131104 | tf_op jit(solution)/shard_map/ppermute | solution.py:159
  110.2 5.4 %collective-permute-done.9 = bf16[128,4,128]{2,0,1:T(8,128)(2,1)S(1)} collective-permute-done((bf16[128,4,128]{2,0,1:T(8,128)(2,1)S(1)}, bf16[128,4,128]{2,0,1:T(8,128)(2,1)S(1)}, u32[]{:S(2)}, u32[]{:S(2)}) %collective-permute-start.9) | collective-permute-done | bytes 131104 | tf_op jit(solution)/shard_map/ppermute | solution.py:159
  115.6 0.4 collective-permute-done.10
  116.0 0.6 gather_fusion.5
  116.7 0.1 select_bitcast_fusion
  116.8 0.3 copy.23
  117.2 1.2 pad_maximum_fusion.1.l_ref
  118.4 49.1 %shard_map.81 = f32[12,128,256]{2,1,0:T(8,128)} custom-call(f32[192]{0:T(256)} %reshape.241.w_ref, f32[1]{0:T(128)} %copy.35.k_ref, f32[12,5,16,256]{3,2,1,0:T(8,128)} %broadcast_in_dim.67.tb_ref, f32[16,6,128,128]{3,2,1,0:T(8,128)} %broadcast_in_dim.70.sb_ref, bf16[16,128,256]{2,1,0:T(8,128)(2,1)} %pad_maximum_fusion.1.l_ref), custom_call_target="tpu_custom_call" | custom-call | flops 7197425664 | bytes 25165824 | tf_op jit(solution)/shard_map/pallas_call | solution.py:113
  167.5 1.9 %copy.24 = f32[12,128,256]{1,2,0:T(8,128)S(1)} copy(f32[12,128,256]{2,1,0:T(8,128)} %shard_map.81) | data formatting | bytes 3145728 | tf_op jit(solution)/shard_map/pallas_call | solution.py:113
  169.4 0.2 copy.25
  169.7 2.3 %collective-permute-done.11 = f32[128,12,128]{2,0,1:T(8,128)S(1)} collective-permute-done((f32[128,12,128]{2,0,1:T(8,128)S(1)}, f32[128,12,128]{2,0,1:T(8,128)S(1)}, u32[]{:S(2)}, u32[]{:S(2)}) %collective-permute-start.11) | collective-permute-done | bytes 786464 | tf_op jit(solution)/shard_map/ppermute | solution.py:137
  172.1 1.6 collective-permute-start.12
  173.7 9.7 %collective-permute-done.12 = f32[64,12,128]{2,0,1:T(8,128)S(1)} collective-permute-done((f32[64,12,128]{2,0,1:T(8,128)S(1)}, f32[64,12,128]{2,0,1:T(8,128)S(1)}, u32[]{:S(2)}, u32[]{:S(2)}) %collective-permute-start.12) | collective-permute-done | bytes 393248 | tf_op jit(solution)/shard_map/ppermute | solution.py:137
  183.3 0.8 bitcast_add_fusion.2
  184.2 0.7 copy.36
  (61 shorter events, 2.4 us)
Async XLA Ops:
  0.6 7.4 %copy-start = (f32[4,48,256]{2,1,0:T(8,128)S(1)}, f32[4,48,256]{2,1,0:T(8,128)}, u32[]{:S(2)}) copy-start(f32[4,48,256]{2,1,0:T(8,128)} %param.11) | copy-start | bytes 589828
  1.5 8.8 %collective-permute-start = (s32[4]{0:T(128)S(1)}, s32[4]{0:T(128)S(1)}, u32[]{:S(2)}, u32[]{:S(2)}) collective-permute-start(s32[4]{0:T(128)S(1)} %get-tuple-element.17), channel_id=1, source_target_pairs={{0,4},{4,8},{8,12},{12,0},{1,5},{5,9},{9,13},{13,1},{2,6},{6,10},{... | collective-permute-start | bytes 56 | tf_op jit(solution)/shard_map/ppermute | solution.py:159
  3.1 7.3 %collective-permute-start.1 = (s32[4]{0:T(128)S(1)}, s32[4]{0:T(128)S(1)}, u32[]{:S(2)}, u32[]{:S(2)}) collective-permute-start(s32[4]{0:T(128)S(1)} %get-tuple-element.19), channel_id=1, source_target_pairs={{0,8},{4,12},{8,0},{12,4},{1,9},{5,13},{9,1},{13,5},{2,10},{6,14},... | collective-permute-start | bytes 56 | tf_op jit(solution)/shard_map/ppermute | solution.py:159
  4.2 6.2 %collective-permute-start.2 = (s32[4]{0:T(128)S(1)}, s32[4]{0:T(128)S(1)}, u32[]{:S(2)}, u32[]{:S(2)}) collective-permute-start(s32[4]{0:T(128)S(1)} %get-tuple-element.18), channel_id=1, source_target_pairs={{0,12},{4,0},{8,4},{12,8},{1,13},{5,1},{9,5},{13,9},{2,14},{6,2},{... | collective-permute-start | bytes 56 | tf_op jit(solution)/shard_map/ppermute | solution.py:159
  13.2 6.5 %collective-permute-start.3 = (bf16[128,4,128]{2,0,1:T(8,128)(2,1)S(1)}, bf16[128,4,128]{2,0,1:T(8,128)(2,1)S(1)}, u32[]{:S(2)}, u32[]{:S(2)}) collective-permute-start(bf16[128,4,128]{2,0,1:T(8,128)(2,1)S(1)} %get-tuple-element.15), channel_id=1, source_target_pairs={{0,4},{4,8},{8,12},{12,0},{1,5},{5,9},{9,13},{13,1},{2,6},{6,10},{... | collective-permute-start | bytes 393224 | tf_op jit(solution)/shard_map/ppermute | solution.py:159
  13.3 10.9 %collective-permute-start.4 = (bf16[128,4,128]{2,0,1:T(8,128)(2,1)S(1)}, bf16[128,4,128]{2,0,1:T(8,128)(2,1)S(1)}, u32[]{:S(2)}, u32[]{:S(2)}) collective-permute-start(bf16[128,4,128]{2,0,1:T(8,128)(2,1)S(1)} %get-tuple-element.14), channel_id=1, source_target_pairs={{0,8},{4,12},{8,0},{12,4},{1,9},{5,13},{9,1},{13,5},{2,10},{6,14},... | collective-permute-start | bytes 393224 | tf_op jit(solution)/shard_map/ppermute | solution.py:159
  16.9 10.3 %collective-permute-start.5 = (bf16[128,4,128]{2,0,1:T(8,128)(2,1)S(1)}, bf16[128,4,128]{2,0,1:T(8,128)(2,1)S(1)}, u32[]{:S(2)}, u32[]{:S(2)}) collective-permute-start(bf16[128,4,128]{2,0,1:T(8,128)(2,1)S(1)} %get-tuple-element.13), channel_id=1, source_target_pairs={{0,12},{4,0},{8,4},{12,8},{1,13},{5,1},{9,5},{13,9},{2,14},{6,2},{... | collective-permute-start | bytes 393224 | tf_op jit(solution)/shard_map/ppermute | solution.py:159
  85.8 2.5 %collective-permute-start.6 = (f32[128,12,128]{2,0,1:T(8,128)S(1)}, f32[128,12,128]{2,0,1:T(8,128)}, u32[]{:S(2)}, u32[]{:S(2)}) collective-permute-start(f32[128,12,128]{2,0,1:T(8,128)S(1)} %dynamic-slice_bitcast_fusion.1), channel_id=1, source_target_pairs={{0,1},{1,0},{2,3},{3,2},{4,5},{5,4},{6,7},{7,6},{8,9},{9,8},{10,11... | collective-permute-start | bytes 2359304 | tf_op jit(solution)/shard_map/ppermute | solution.py:137
  85.9 14.9 %copy-start.1 = (bf16[128,12,128]{2,0,1:T(8,128)(2,1)S(1)}, bf16[128,12,128]{2,0,1:T(8,128)(2,1)}, u32[]{:S(2)}) copy-start(bf16[128,12,128]{2,0,1:T(8,128)(2,1)} %param.10) | copy-start | bytes 1179652
  89.5 11.2 %collective-permute-start.7 = (f32[64,12,128]{2,0,1:T(8,128)S(1)}, f32[64,12,128]{2,0,1:T(8,128)S(1)}, u32[]{:S(2)}, u32[]{:S(2)}) collective-permute-start(f32[64,12,128]{2,0,1:T(8,128)S(1)} %dynamic-slice_bitcast_fusion.3), channel_id=1, source_target_pairs={{0,2},{2,0},{1,3},{3,1},{4,6},{6,4},{5,7},{7,5},{8,10},{10,8},{9,1... | collective-permute-start | bytes 1179656 | tf_op jit(solution)/shard_map/ppermute | solution.py:137
  103.8 6.4 %collective-permute-start.8 = (bf16[128,4,128]{2,0,1:T(8,128)(2,1)S(1)}, bf16[128,4,128]{2,0,1:T(8,128)(2,1)S(1)}, u32[]{:S(2)}, u32[]{:S(2)}) collective-permute-start(bf16[128,4,128]{2,0,1:T(8,128)(2,1)S(1)} %get-tuple-element.9), channel_id=1, source_target_pairs={{0,4},{4,8},{8,12},{12,0},{1,5},{5,9},{9,13},{13,1},{2,6},{6,10},{... | collective-permute-start | bytes 393224 | tf_op jit(solution)/shard_map/ppermute | solution.py:159
  103.8 11.8 %collective-permute-start.9 = (bf16[128,4,128]{2,0,1:T(8,128)(2,1)S(1)}, bf16[128,4,128]{2,0,1:T(8,128)(2,1)S(1)}, u32[]{:S(2)}, u32[]{:S(2)}) collective-permute-start(bf16[128,4,128]{2,0,1:T(8,128)(2,1)S(1)} %get-tuple-element.8), channel_id=1, source_target_pairs={{0,8},{4,12},{8,0},{12,4},{1,9},{5,13},{9,1},{13,5},{2,10},{6,14},... | collective-permute-start | bytes 393224 | tf_op jit(solution)/shard_map/ppermute | solution.py:159
  103.9 12.0 %collective-permute-start.10 = (bf16[128,4,128]{2,0,1:T(8,128)(2,1)S(1)}, bf16[128,4,128]{2,0,1:T(8,128)(2,1)S(1)}, u32[]{:S(2)}, u32[]{:S(2)}) collective-permute-start(bf16[128,4,128]{2,0,1:T(8,128)(2,1)S(1)} %get-tuple-element.7), channel_id=1, source_target_pairs={{0,12},{4,0},{8,4},{12,8},{1,13},{5,1},{9,5},{13,9},{2,14},{6,2},{... | collective-permute-start | bytes 393224 | tf_op jit(solution)/shard_map/ppermute | solution.py:159
  169.6 2.4 %collective-permute-start.11 = (f32[128,12,128]{2,0,1:T(8,128)S(1)}, f32[128,12,128]{2,0,1:T(8,128)S(1)}, u32[]{:S(2)}, u32[]{:S(2)}) collective-permute-start(f32[128,12,128]{2,0,1:T(8,128)S(1)} %dynamic-slice_bitcast_fusion), channel_id=1, source_target_pairs={{0,1},{1,0},{2,3},{3,2},{4,5},{5,4},{6,7},{7,6},{8,9},{9,8},{10,11... | collective-permute-start | bytes 2359304 | tf_op jit(solution)/shard_map/ppermute | solution.py:137
  172.1 11.2 %collective-permute-start.12 = (f32[64,12,128]{2,0,1:T(8,128)S(1)}, f32[64,12,128]{2,0,1:T(8,128)S(1)}, u32[]{:S(2)}, u32[]{:S(2)}) collective-permute-start(f32[64,12,128]{2,0,1:T(8,128)S(1)} %dynamic-slice_bitcast_fusion.2), channel_id=1, source_target_pairs={{0,2},{2,0},{1,3},{3,1},{4,6},{6,4},{5,7},{7,5},{8,10},{10,8},{9,1... | collective-permute-start | bytes 1179656 | tf_op jit(solution)/shard_map/ppermute | solution.py:137
where the time goes:
time: 185 us
  Pallas kernels  98.3 us (53%)
  waiting for transfers between devices  43.6 us (24%)
  local copies, waits for them, and re-layouts  18.2 us (10%)
  starting transfers between devices  13.7 us (7%)
  other arithmetic  7.31 us (4%)
  blocking collectives  2.09 us (1%)
    pallas_call x2, Pallas kernels, product(): pl.pallas_call(product_kernel, out_shape=jax.ShapeDtypeStruct((clusters,...  98.3 us
    ppermute x4, waiting for transfers between devices, scatter_sum(): total = total + lax.ppermute(send, axis, perm=perm)  24 us
    ppermute x9, waiting for transfers between devices, swap_chunks(): by_shift.append(lax.ppermute(send, 'clus', perm=perm))  19.6 us
    ppermute x9, starting transfers between devices, swap_chunks(): by_shift.append(lax.ppermute(send, 'clus', perm=perm))  10.4 us
    broadcast_in_dim x1, local copies, waits for them, and re-layouts, local(): sb = jnp.broadcast_to(sq[..., None], sq.shape + (LANES,))  3.8 us
    pallas_call x2, local copies, waits for them, and re-layouts, product(): pl.pallas_call(product_kernel, out_shape=jax.ShapeDtypeStruct((clusters,...  3.73 us
  transfers between devices with their start and end apart: 13, of which 10 were waited for; matrix products, arithmetic and copies ran while one was open for 2% of the time, Pallas kernels for 0%

commit v1 on v0

--- a/solution.py
+++ b/solution.py
@@ -24,7 +24,6 @@
 
 STRIP = 16
 LANES = 128
-UNROLL = 4
 
 
 def green(k, xt, yt, zt, zt4, et, xs, ys, zs, area, sj, cj):
@@ -71,33 +70,45 @@
             ti_ref[rows, lanes] = im.astype(jnp.bfloat16)
         return carry
 
-    lax.fori_loop(0, width // STRIP, strip, 0, unroll=UNROLL)
+    for r in range(width // STRIP):
+        strip(r, 0)
 
 
 def entry_product(l_ref, p, tile):
     return jnp.dot(l_ref[p], tile, preferred_element_type=jnp.float32)
 
 
-def product_kernel(w_ref, k_ref, tb_ref, sb_ref, l_ref, acc_ref, tbuf):
+def product_kernel(w_ref, k_ref, tb_ref, sb_ref, l_ref, acc_ref, tbuf, idx_ref):
     k = k_ref[0]
     slots = sb_ref.shape[0]
-    width = tbuf.shape[0] // 2
+    width = tbuf.shape[1] // 2
     acc_ref[...] = jnp.zeros_like(acc_ref)
 
-    def body(e, carry):
-        w = w_ref[e]
-
-        @pl.when(w > 0.0)
-        def _():
+    def gather(e, n):
+        idx_ref[n] = e
+        return n + (w_ref[e] > 0.0).astype(jnp.int32)
+
+    n = lax.fori_loop(0, w_ref.shape[0], gather, 0)
+
+    def build(e, slot):
+        tile_into(k, tb_ref, sb_ref, e // slots, e % slots, tbuf.at[slot, pl.ds(0, width)],
+                  tbuf.at[slot, pl.ds(width, width)])
+
+    @pl.when(n > 0)
+    def _():
+        build(idx_ref[0], 0)
+
+        def body(i, carry):
+            e = idx_ref[i]
+            nxt = idx_ref[jnp.minimum(i + 1, n - 1)]
+            slot = i % 2
+            build(nxt, 1 - slot)
             g = e // slots
-            p = e % slots
-            tile_into(k, tb_ref, sb_ref, g, p, tbuf.at[pl.ds(0, width)], tbuf.at[pl.ds(width, width)])
-            part = entry_product(l_ref, p, tbuf[...])
-            acc_ref[g] = acc_ref[g] + w * part
-
-        return carry
-
-    lax.fori_loop(0, w_ref.shape[0], body, 0)
+            part = entry_product(l_ref, e % slots, tbuf[slot])
+            acc_ref[g] = acc_ref[g] + w_ref[e] * part
+            return carry
+
+        lax.fori_loop(0, n, body, 0)
 
 
 SMEM_SPEC = pl.BlockSpec(memory_space=pltpu.SMEM)
@@ -115,7 +126,10 @@
         out_shape=jax.ShapeDtypeStruct((clusters, cols, targets), jnp.float32),
         in_specs=[SMEM_SPEC] * 2 + [VMEM_SPEC] * 3,
         out_specs=VMEM_SPEC,
-        scratch_shapes=[pltpu.VMEM((2 * width, targets), jnp.bfloat16)],
+        scratch_shapes=[
+            pltpu.VMEM((2, 2 * width, targets), jnp.bfloat16),
+            pltpu.SMEM((w_list.shape[0],), jnp.int32),
+        ],
         cost_estimate=pl.CostEstimate(
             flops=elems * 60 + 4 * elems * cols,
             transcendentals=elems * 4,

time: 185 us -> 183 us (0.989)
  starting transfers between devices: 13.7 us -> 76.4 us
  Pallas kernels: 98.3 us -> 35.7 us
    ppermute x4, starting transfers between devices: 3.26 us -> 65.9 us  [scatter_sum(): total = total + lax.ppermute(send, axis, perm=perm)]
    pallas_call x2, Pallas kernels: 98.3 us -> 35.7 us  [product(): pl.pallas_call(product_kernel, out_shape=jax.ShapeDtypeStruct((clusters,...]
where the time goes in v1:
time: 183 us; the launch traced here: 185 us
  starting transfers between devices  76.4 us (42%)
  waiting for transfers between devices  43.4 us (24%)
  Pallas kernels  35.7 us (20%)
  local copies, waits for them, and re-layouts  18.2 us (10%)
  other arithmetic  7.31 us (4%)
  blocking collectives  2.09 us (1%)
    ppermute x4, starting transfers between devices, scatter_sum(): total = total + lax.ppermute(send, axis, perm=perm)  65.9 us
    pallas_call x2, Pallas kernels, product(): pl.pallas_call(product_kernel, out_shape=jax.ShapeDtypeStruct((clusters,...  35.7 us
    ppermute x4, waiting for transfers between devices, scatter_sum(): total = total + lax.ppermute(send, axis, perm=perm)  23.7 us
    ppermute x9, waiting for transfers between devices, swap_chunks(): by_shift.append(lax.ppermute(send, 'clus', perm=perm))  19.6 us
    ppermute x9, starting transfers between devices, swap_chunks(): by_shift.append(lax.ppermute(send, 'clus', perm=perm))  10.4 us
    broadcast_in_dim x1, local copies, waits for them, and re-layouts, local(): sb = jnp.broadcast_to(sq[..., None], sq.shape + (LANES,))  3.8 us
    pallas_call x2, local copies, waits for them, and re-layouts, product(): pl.pallas_call(product_kernel, out_shape=jax.ShapeDtypeStruct((clusters,...  3.73 us
  transfers between devices with their start and end apart: 13, of which 10 were waited for; matrix products, arithmetic and copies ran while one was open for 2% of the time, Pallas kernels for 0%

profile of v1, /device:TPU:8, one launch (start us, length us, event | category | flops | bytes accessed | tf_op | source)
XLA Modules:
  0.0 184.7 jit_solution(17710841125086927582)
XLA Ops:
  0.7 0.8 fusion.11
  1.5 1.6 collective-permute-start
  3.1 1.1 collective-permute-start.1
  4.2 2.0 %collective-permute-start.2 = (s32[4]{0:T(128)S(1)}, s32[4]{0:T(128)S(1)}, u32[]{:S(2)}, u32[]{:S(2)}) collective-permute-start(s32[4]{0:T(128)S(1)} %get-tuple-element.18), channel_id=1, source_target_pairs={{0,12},{4,0},{8,4},{12,8},{1,13},{5,1},{9,5},{13,9},{2,14},{6,2},{... | collective-permute-start | bytes 56 | tf_op jit(solution)/shard_map/ppermute | solution.py:173
  6.2 0.7 broadcast_maximum_fusion
  8.2 0.7 copy.28
  8.9 0.7 iota_compare_fusion.1
  9.7 0.6 reshape.241.w_ref
  10.4 0.6 gather_fusion.1
  11.3 1.6 gather_fusion.2
  13.0 0.1 bitcast_multiply_fusion.1
  13.3 3.6 %collective-permute-start.4 = (bf16[128,4,128]{2,0,1:T(8,128)(2,1)S(1)}, bf16[128,4,128]{2,0,1:T(8,128)(2,1)S(1)}, u32[]{:S(2)}, u32[]{:S(2)}) collective-permute-start(bf16[128,4,128]{2,0,1:T(8,128)(2,1)S(1)} %get-tuple-element.14), channel_id=1, source_target_pairs={{0,8},{4,12},{8,0},{12,4},{1,9},{5,13},{9,1},{13,5},{2,10},{6,14},... | collective-permute-start | bytes 393224 | tf_op jit(solution)/shard_map/ppermute | solution.py:173
  16.9 0.6 gather_fusion
  17.8 1.9 %collective-permute-done.3 = bf16[128,4,128]{2,0,1:T(8,128)(2,1)S(1)} collective-permute-done((bf16[128,4,128]{2,0,1:T(8,128)(2,1)S(1)}, bf16[128,4,128]{2,0,1:T(8,128)(2,1)S(1)}, u32[]{:S(2)}, u32[]{:S(2)}) %collective-permute-start.3) | collective-permute-done | bytes 131104 | tf_op jit(solution)/shard_map/ppermute | solution.py:173
  19.7 4.5 %collective-permute-done.4 = bf16[128,4,128]{2,0,1:T(8,128)(2,1)S(1)} collective-permute-done((bf16[128,4,128]{2,0,1:T(8,128)(2,1)S(1)}, bf16[128,4,128]{2,0,1:T(8,128)(2,1)S(1)}, u32[]{:S(2)}, u32[]{:S(2)}) %collective-permute-start.4) | collective-permute-done | bytes 131104 | tf_op jit(solution)/shard_map/ppermute | solution.py:173
  24.2 3.1 %collective-permute-done.5 = bf16[128,4,128]{2,0,1:T(8,128)(2,1)S(1)} collective-permute-done((bf16[128,4,128]{2,0,1:T(8,128)(2,1)S(1)}, bf16[128,4,128]{2,0,1:T(8,128)(2,1)S(1)}, u32[]{:S(2)}, u32[]{:S(2)}) %collective-permute-start.5) | collective-permute-done | bytes 131104 | tf_op jit(solution)/shard_map/ppermute | solution.py:173
  27.4 0.6 gather_fusion.3
  28.1 0.3 copy.20
  28.5 1.2 pad_maximum_fusion.l_ref
  29.7 3.8 %broadcast_in_dim.70.sb_ref = f32[16,6,128,128]{3,2,1,0:T(8,128)} broadcast(f32[16,6,128]{2,1,0:T(8,128)S(1)} %copy.19), dimensions={0,1,2} | broadcast | bytes 6340608 | tf_op jit(solution)/shard_map/broadcast_in_dim | solution.py:211
  33.5 1.0 broadcast_in_dim.67.tb_ref
  34.5 17.8 %shard_map.80 = f32[12,128,256]{2,1,0:T(8,128)} custom-call(f32[192]{0:T(256)} %reshape.241.w_ref, f32[1]{0:T(128)} %copy.35.k_ref, f32[12,5,16,256]{3,2,1,0:T(8,128)} %broadcast_in_dim.67.tb_ref, f32[16,6,128,128]{3,2,1,0:T(8,128)} %broadcast_in_dim.70.sb_ref, bf16[16,128,256]{2,1,0:T(8,128)(2,1)} %pad_maximum_fusion.l_ref), custom_call_target="tpu_custom_call" | custom-call | flops 7197425664 | bytes 25165824 | tf_op jit(solution)/shard_map/pallas_call | solution.py:124
  52.4 1.9 %copy.21 = f32[12,128,256]{1,2,0:T(8,128)S(1)} copy(f32[12,128,256]{2,1,0:T(8,128)} %shard_map.80) | data formatting | bytes 3145728 | tf_op jit(solution)/shard_map/pallas_call | solution.py:124
  54.2 0.2 copy.22
  54.5 31.1 %collective-permute-start.6 = (f32[128,12,128]{2,0,1:T(8,128)S(1)}, f32[128,12,128]{2,0,1:T(8,128)}, u32[]{:S(2)}, u32[]{:S(2)}) collective-permute-start(f32[128,12,128]{2,0,1:T(8,128)S(1)} %dynamic-slice_bitcast_fusion.1), channel_id=1, source_target_pairs={{0,1},{1,0},{2,3},{3,2},{4,5},{5,4},{6,7},{7,6},{8,9},{9,8},{10,11... | collective-permute-start | bytes 2359304 | tf_op jit(solution)/shard_map/ppermute | solution.py:151
  85.6 2.0 %collective-permute-done.6 = f32[128,12,128]{2,0,1:T(8,128)} collective-permute-done((f32[128,12,128]{2,0,1:T(8,128)S(1)}, f32[128,12,128]{2,0,1:T(8,128)}, u32[]{:S(2)}, u32[]{:S(2)}) %collective-permute-start.6) | collective-permute-done | bytes 786464 | tf_op jit(solution)/shard_map/ppermute | solution.py:151
  87.6 1.2 bitcast_add_fusion.1
  88.9 1.6 collective-permute-start.7
  90.5 9.9 %collective-permute-done.7 = f32[64,12,128]{2,0,1:T(8,128)S(1)} collective-permute-done((f32[64,12,128]{2,0,1:T(8,128)S(1)}, f32[64,12,128]{2,0,1:T(8,128)S(1)}, u32[]{:S(2)}, u32[]{:S(2)}) %collective-permute-start.7) | collective-permute-done | bytes 393248 | tf_op jit(solution)/shard_map/ppermute | solution.py:151
  100.4 2.1 %all_gather.3 = bf16[128,12,128]{2,0,1:T(8,128)(2,1)S(1)} all-gather(bf16[64,12,128]{2,0,1:T(8,128)(2,1)S(1)} %fusion.1), channel_id=1, replica_groups=mesh['freq'=2,'clus'=4,'src'=2,'sub'=2] {'sub'}, dimensions={0}, use_global_device_ids=true | all-gather | bytes 589824 | tf_op jit(solution)/shard_map/all_gather | solution.py:233
  102.5 0.6 gather_fusion.4
  103.2 0.1 bitcast_multiply_fusion
  103.5 1.9 %collective-permute-start.10 = (bf16[128,4,128]{2,0,1:T(8,128)(2,1)S(1)}, bf16[128,4,128]{2,0,1:T(8,128)(2,1)S(1)}, u32[]{:S(2)}, u32[]{:S(2)}) collective-permute-start(bf16[128,4,128]{2,0,1:T(8,128)(2,1)S(1)} %get-tuple-element.7), channel_id=1, source_target_pairs={{0,12},{4,0},{8,4},{12,8},{1,13},{5,1},{9,5},{13,9},{2,14},{6,2},{... | collective-permute-start | bytes 393224 | tf_op jit(solution)/shard_map/ppermute | solution.py:173
  105.5 4.3 %collective-permute-done.8 = bf16[128,4,128]{2,0,1:T(8,128)(2,1)S(1)} collective-permute-done((bf16[128,4,128]{2,0,1:T(8,128)(2,1)S(1)}, bf16[128,4,128]{2,0,1:T(8,128)(2,1)S(1)}, u32[]{:S(2)}, u32[]{:S(2)}) %collective-permute-start.8) | collective-permute-done | bytes 131104 | tf_op jit(solution)/shard_map/ppermute | solution.py:173
  109.8 5.4 %collective-permute-done.9 = bf16[128,4,128]{2,0,1:T(8,128)(2,1)S(1)} collective-permute-done((bf16[128,4,128]{2,0,1:T(8,128)(2,1)S(1)}, bf16[128,4,128]{2,0,1:T(8,128)(2,1)S(1)}, u32[]{:S(2)}, u32[]{:S(2)}) %collective-permute-start.9) | collective-permute-done | bytes 131104 | tf_op jit(solution)/shard_map/ppermute | solution.py:173
  115.2 0.4 collective-permute-done.10
  115.6 0.6 gather_fusion.5
  116.4 0.3 copy.23
  116.8 1.2 pad_maximum_fusion.1.l_ref
  118.0 17.8 %shard_map.81 = f32[12,128,256]{2,1,0:T(8,128)} custom-call(f32[192]{0:T(256)} %reshape.241.w_ref, f32[1]{0:T(128)} %copy.35.k_ref, f32[12,5,16,256]{3,2,1,0:T(8,128)} %broadcast_in_dim.67.tb_ref, f32[16,6,128,128]{3,2,1,0:T(8,128)} %broadcast_in_dim.70.sb_ref, bf16[16,128,256]{2,1,0:T(8,128)(2,1)} %pad_maximum_fusion.1.l_ref), custom_call_target="tpu_custom_call" | custom-call | flops 7197425664 | bytes 25165824 | tf_op jit(solution)/shard_map/pallas_call | solution.py:124
  135.8 1.9 %copy.24 = f32[12,128,256]{1,2,0:T(8,128)S(1)} copy(f32[12,128,256]{2,1,0:T(8,128)} %shard_map.81) | data formatting | bytes 3145728 | tf_op jit(solution)/shard_map/pallas_call | solution.py:124
  137.7 0.2 copy.25
  137.9 31.7 %collective-permute-start.11 = (f32[128,12,128]{2,0,1:T(8,128)S(1)}, f32[128,12,128]{2,0,1:T(8,128)S(1)}, u32[]{:S(2)}, u32[]{:S(2)}) collective-permute-start(f32[128,12,128]{2,0,1:T(8,128)S(1)} %dynamic-slice_bitcast_fusion), channel_id=1, source_target_pairs={{0,1},{1,0},{2,3},{3,2},{4,5},{5,4},{6,7},{7,6},{8,9},{9,8},{10,11... | collective-permute-start | bytes 2359304 | tf_op jit(solution)/shard_map/ppermute | solution.py:151
  169.6 1.9 %collective-permute-done.11 = f32[128,12,128]{2,0,1:T(8,128)S(1)} collective-permute-done((f32[128,12,128]{2,0,1:T(8,128)S(1)}, f32[128,12,128]{2,0,1:T(8,128)S(1)}, u32[]{:S(2)}, u32[]{:S(2)}) %collective-permute-start.11) | collective-permute-done | bytes 786464 | tf_op jit(solution)/shard_map/ppermute | solution.py:151
  171.7 1.6 collective-permute-start.12
  173.2 9.9 %collective-permute-done.12 = f32[64,12,128]{2,0,1:T(8,128)S(1)} collective-permute-done((f32[64,12,128]{2,0,1:T(8,128)S(1)}, f32[64,12,128]{2,0,1:T(8,128)S(1)}, u32[]{:S(2)}, u32[]{:S(2)}) %collective-permute-start.12) | collective-permute-done | bytes 393248 | tf_op jit(solution)/shard_map/ppermute | solution.py:151
  183.1 0.8 bitcast_add_fusion.2
  183.9 0.7 copy.36
  (61 shorter events, 2.5 us)
Async XLA Ops:
  0.6 7.4 %copy-start = (f32[4,48,256]{2,1,0:T(8,128)S(1)}, f32[4,48,256]{2,1,0:T(8,128)}, u32[]{:S(2)}) copy-start(f32[4,48,256]{2,1,0:T(8,128)} %param.11) | copy-start | bytes 589828
  1.5 8.8 %collective-permute-start = (s32[4]{0:T(128)S(1)}, s32[4]{0:T(128)S(1)}, u32[]{:S(2)}, u32[]{:S(2)}) collective-permute-start(s32[4]{0:T(128)S(1)} %get-tuple-element.17), channel_id=1, source_target_pairs={{0,4},{4,8},{8,12},{12,0},{1,5},{5,9},{9,13},{13,1},{2,6},{6,10},{... | collective-permute-start | bytes 56 | tf_op jit(solution)/shard_map/ppermute | solution.py:173
  3.1 7.3 %collective-permute-start.1 = (s32[4]{0:T(128)S(1)}, s32[4]{0:T(128)S(1)}, u32[]{:S(2)}, u32[]{:S(2)}) collective-permute-start(s32[4]{0:T(128)S(1)} %get-tuple-element.19), channel_id=1, source_target_pairs={{0,8},{4,12},{8,0},{12,4},{1,9},{5,13},{9,1},{13,5},{2,10},{6,14},... | collective-permute-start | bytes 56 | tf_op jit(solution)/shard_map/ppermute | solution.py:173
  4.2 6.2 %collective-permute-start.2 = (s32[4]{0:T(128)S(1)}, s32[4]{0:T(128)S(1)}, u32[]{:S(2)}, u32[]{:S(2)}) collective-permute-start(s32[4]{0:T(128)S(1)} %get-tuple-element.18), channel_id=1, source_target_pairs={{0,12},{4,0},{8,4},{12,8},{1,13},{5,1},{9,5},{13,9},{2,14},{6,2},{... | collective-permute-start | bytes 56 | tf_op jit(solution)/shard_map/ppermute | solution.py:173
  13.2 6.5 %collective-permute-start.3 = (bf16[128,4,128]{2,0,1:T(8,128)(2,1)S(1)}, bf16[128,4,128]{2,0,1:T(8,128)(2,1)S(1)}, u32[]{:S(2)}, u32[]{:S(2)}) collective-permute-start(bf16[128,4,128]{2,0,1:T(8,128)(2,1)S(1)} %get-tuple-element.15), channel_id=1, source_target_pairs={{0,4},{4,8},{8,12},{12,0},{1,5},{5,9},{9,13},{13,1},{2,6},{6,10},{... | collective-permute-start | bytes 393224 | tf_op jit(solution)/shard_map/ppermute | solution.py:173
  13.3 10.9 %collective-permute-start.4 = (bf16[128,4,128]{2,0,1:T(8,128)(2,1)S(1)}, bf16[128,4,128]{2,0,1:T(8,128)(2,1)S(1)}, u32[]{:S(2)}, u32[]{:S(2)}) collective-permute-start(bf16[128,4,128]{2,0,1:T(8,128)(2,1)S(1)} %get-tuple-element.14), channel_id=1, source_target_pairs={{0,8},{4,12},{8,0},{12,4},{1,9},{5,13},{9,1},{13,5},{2,10},{6,14},... | collective-permute-start | bytes 393224 | tf_op jit(solution)/shard_map/ppermute | solution.py:173
  16.9 10.3 %collective-permute-start.5 = (bf16[128,4,128]{2,0,1:T(8,128)(2,1)S(1)}, bf16[128,4,128]{2,0,1:T(8,128)(2,1)S(1)}, u32[]{:S(2)}, u32[]{:S(2)}) collective-permute-start(bf16[128,4,128]{2,0,1:T(8,128)(2,1)S(1)} %get-tuple-element.13), channel_id=1, source_target_pairs={{0,12},{4,0},{8,4},{12,8},{1,13},{5,1},{9,5},{13,9},{2,14},{6,2},{... | collective-permute-start | bytes 393224 | tf_op jit(solution)/shard_map/ppermute | solution.py:173
  54.5 33.2 %collective-permute-start.6 = (f32[128,12,128]{2,0,1:T(8,128)S(1)}, f32[128,12,128]{2,0,1:T(8,128)}, u32[]{:S(2)}, u32[]{:S(2)}) collective-permute-start(f32[128,12,128]{2,0,1:T(8,128)S(1)} %dynamic-slice_bitcast_fusion.1), channel_id=1, source_target_pairs={{0,1},{1,0},{2,3},{3,2},{4,5},{5,4},{6,7},{7,6},{8,9},{9,8},{10,11... | collective-permute-start | bytes 2359304 | tf_op jit(solution)/shard_map/ppermute | solution.py:151
  85.6 14.8 %copy-start.1 = (bf16[128,12,128]{2,0,1:T(8,128)(2,1)S(1)}, bf16[128,12,128]{2,0,1:T(8,128)(2,1)}, u32[]{:S(2)}) copy-start(bf16[128,12,128]{2,0,1:T(8,128)(2,1)} %param.10) | copy-start | bytes 1179652
  88.9 11.5 %collective-permute-start.7 = (f32[64,12,128]{2,0,1:T(8,128)S(1)}, f32[64,12,128]{2,0,1:T(8,128)S(1)}, u32[]{:S(2)}, u32[]{:S(2)}) collective-permute-start(f32[64,12,128]{2,0,1:T(8,128)S(1)} %dynamic-slice_bitcast_fusion.3), channel_id=1, source_target_pairs={{0,2},{2,0},{1,3},{3,1},{4,6},{6,4},{5,7},{7,5},{8,10},{10,8},{9,1... | collective-permute-start | bytes 1179656 | tf_op jit(solution)/shard_map/ppermute | solution.py:151
  103.4 6.4 %collective-permute-start.8 = (bf16[128,4,128]{2,0,1:T(8,128)(2,1)S(1)}, bf16[128,4,128]{2,0,1:T(8,128)(2,1)S(1)}, u32[]{:S(2)}, u32[]{:S(2)}) collective-permute-start(bf16[128,4,128]{2,0,1:T(8,128)(2,1)S(1)} %get-tuple-element.9), channel_id=1, source_target_pairs={{0,4},{4,8},{8,12},{12,0},{1,5},{5,9},{9,13},{13,1},{2,6},{6,10},{... | collective-permute-start | bytes 393224 | tf_op jit(solution)/shard_map/ppermute | solution.py:173
  103.5 11.8 %collective-permute-start.9 = (bf16[128,4,128]{2,0,1:T(8,128)(2,1)S(1)}, bf16[128,4,128]{2,0,1:T(8,128)(2,1)S(1)}, u32[]{:S(2)}, u32[]{:S(2)}) collective-permute-start(bf16[128,4,128]{2,0,1:T(8,128)(2,1)S(1)} %get-tuple-element.8), channel_id=1, source_target_pairs={{0,8},{4,12},{8,0},{12,4},{1,9},{5,13},{9,1},{13,5},{2,10},{6,14},... | collective-permute-start | bytes 393224 | tf_op jit(solution)/shard_map/ppermute | solution.py:173
  103.5 12.0 %collective-permute-start.10 = (bf16[128,4,128]{2,0,1:T(8,128)(2,1)S(1)}, bf16[128,4,128]{2,0,1:T(8,128)(2,1)S(1)}, u32[]{:S(2)}, u32[]{:S(2)}) collective-permute-start(bf16[128,4,128]{2,0,1:T(8,128)(2,1)S(1)} %get-tuple-element.7), channel_id=1, source_target_pairs={{0,12},{4,0},{8,4},{12,8},{1,13},{5,1},{9,5},{13,9},{2,14},{6,2},{... | collective-permute-start | bytes 393224 | tf_op jit(solution)/shard_map/ppermute | solution.py:173
  137.9 33.6 %collective-permute-start.11 = (f32[128,12,128]{2,0,1:T(8,128)S(1)}, f32[128,12,128]{2,0,1:T(8,128)S(1)}, u32[]{:S(2)}, u32[]{:S(2)}) collective-permute-start(f32[128,12,128]{2,0,1:T(8,128)S(1)} %dynamic-slice_bitcast_fusion), channel_id=1, source_target_pairs={{0,1},{1,0},{2,3},{3,2},{4,5},{5,4},{6,7},{7,6},{8,9},{9,8},{10,11... | collective-permute-start | bytes 2359304 | tf_op jit(solution)/shard_map/ppermute | solution.py:151
  171.7 11.5 %collective-permute-start.12 = (f32[64,12,128]{2,0,1:T(8,128)S(1)}, f32[64,12,128]{2,0,1:T(8,128)S(1)}, u32[]{:S(2)}, u32[]{:S(2)}) collective-permute-start(f32[64,12,128]{2,0,1:T(8,128)S(1)} %dynamic-slice_bitcast_fusion.2), channel_id=1, source_target_pairs={{0,2},{2,0},{1,3},{3,1},{4,6},{6,4},{5,7},{7,5},{8,10},{10,8},{9,1... | collective-permute-start | bytes 1179656 | tf_op jit(solution)/shard_map/ppermute | solution.py:151
